TPU v7x, 512 devices: a whole 4x8x8 slice. The times are simulated.
512 devices in a mesh: section: 8 (over y), dp: 64 (over x, z, core).
Axes of the slice: x: 4, y: 8, z: 8, core: 2. Of those that a mesh axis runs over, the one named last changes fastest.
Arguments:
- queries: bfloat16 [65536, 3584], P(('section', 'dp')), may hold values from -1 to 1
- passages: bfloat16 [128, 64, 3584], P('dp'), may hold values from -1 to 1
- candidates: int32 [512, 3], P('section'), may hold values from 0 to 63, as said below
- counts: int32 [512], P('section'), may hold values from 1 to 3, 1024 in all
- teacher: float32 [65536, 384], P(('section', 'dp')), may hold values from -20 to 450
- section_weights: bfloat16 [8, 3584, 3584], P('section', 'dp'), may hold values from -0.09375 to 0.09375
- section_inputs: bfloat16 [8, 64, 3584], P('section', None, 'dp'), may hold values from -1.5 to 1.5
- pre_acts: bfloat16 [8, 64, 3584], P('section', None, 'dp'), may hold values from -8 to 8
Outputs:
- query_grads: bfloat16 [65536, 3584], P(('section', 'dp'))
- passage_grads: bfloat16 [128, 64, 3584], P('dp')
- grad_inputs: float32 [8, 64, 3584], P('section', None, 'dp')
- weight_grads: bfloat16 [8, 3584, 3584], P('section', 'dp')
Inputs may be any that keep to these rules, and one draw needn't show every extreme that they name: `candidates`: each row names 3 different passage blocks. A query block uses the first counts[b] entries of its row of candidates.
All inputs are finite; a program needn't handle non-finite values.
Results may differ from a plain program's by a relative error of at most 0.0085.
Values may be sent and summed in bfloat16 or wider, within the bound.
No kernel may reach another device: no remote copies, remote signals or barrier semaphores. Data moves between devices by JAX's collectives and lax.ppermute only.
A program may use at most 64 MiB of HBM per device.

v0:
```python
import jax
import jax.numpy as jnp
from jax import lax
from jax.sharding import PartitionSpec as P

INVERSE_TEMP = 20.0


def passed_along(value, axis, steps):
    count = lax.axis_size(axis)
    initial, last = (max(0, -steps), min(count, count - steps))
    return lax.ppermute(value, axis, [(source, source + steps) for source in range(initial, last)])


def soft_weights(logits, valid):
    masked = jnp.where(valid, logits, -1e30)
    highest = jnp.max(masked, axis=-1, keepdims=True)
    expons = jnp.where(valid, jnp.exp(masked - highest), 0.0)
    return expons / jnp.sum(expons, axis=-1, keepdims=True)


def body(queries, passages, candidates, counts, teacher, section_weights, section_inputs, pre_acts):
    dp_count = lax.axis_size("dp")
    dp_index = lax.axis_index("dp")
    stripe, block_total, width = passages.shape
    row_block_count = stripe * dp_count
    blocks_here = candidates.shape[0] // dp_count
    slot_count = candidates.shape[1]
    requests = blocks_here * slot_count
    all_slots = candidates.reshape(-1)
    outgoing = jnp.take(passages, all_slots, axis=1)
    pulled_rows = lax.all_to_all(outgoing, "dp", split_axis=1, concat_axis=0, tiled=True)
    pulled_rows = pulled_rows.reshape(row_block_count, blocks_here, slot_count, width)
    own_counts = lax.dynamic_slice_in_dim(counts, dp_index * blocks_here, blocks_here)
    slot_valid = jnp.arange(slot_count, dtype=jnp.int32)[None, :] < own_counts[:, None]
    column_valid = jnp.repeat(slot_valid, row_block_count, axis=1)[:, None, :]
    query_row_items = queries.reshape(blocks_here, row_block_count, width)
    logits = (
        jnp.einsum(
            "ixp,wifp->ixfw", query_row_items, pulled_rows, preferred_element_type=jnp.float32
        )
        * INVERSE_TEMP
    )
    logits = logits.reshape(blocks_here, row_block_count, slot_count * row_block_count)
    target_logits = soft_weights(
        teacher.reshape(blocks_here, row_block_count, slot_count * row_block_count), column_valid
    )
    weight_matrices = (soft_weights(logits, column_valid) - target_logits).astype(jnp.bfloat16)
    weight_matrices = weight_matrices.reshape(
        blocks_here, row_block_count, slot_count, row_block_count
    )
    query_sums = (
        jnp.einsum(
            "geal,lgay->gey", weight_matrices, pulled_rows, preferred_element_type=jnp.float32
        )
        * INVERSE_TEMP
    )
    passage_sums = (
        jnp.einsum(
            "fnyw,fnj->wfyj", weight_matrices, query_row_items, preferred_element_type=jnp.float32
        )
        * INVERSE_TEMP
    )
    block_terms = passage_sums.reshape(row_block_count, requests, width).astype(jnp.bfloat16)
    micro_count = section_inputs.shape[1] // dp_count
    col_width = width // dp_count
    micro_cols = jnp.transpose(
        query_sums[0, :micro_count].reshape(micro_count, dp_count, col_width), (1, 0, 2)
    )
    incoming_piece = lax.all_to_all(block_terms, "dp", split_axis=0, concat_axis=1, tiled=True)
    entry = lax.all_to_all(micro_cols, "dp", split_axis=0, concat_axis=1, tiled=True)
    onehot = (all_slots[:, None] == jnp.arange(block_total, dtype=jnp.int32)[None, :]).astype(
        jnp.float32
    )
    dense = jnp.einsum(
        "sjd,jn->snd",
        incoming_piece.astype(jnp.float32),
        onehot,
        precision=lax.Precision.HIGHEST,
        preferred_element_type=jnp.float32,
    )
    passage_out = lax.psum(dense, "section").astype(jnp.bfloat16)
    weight_rows = section_weights[0]
    input_cols = section_inputs[0]
    pre = pre_acts[0].astype(jnp.float32)
    sigma = jax.nn.sigmoid(pre)
    slope = sigma * (1.0 + pre * (1.0 - sigma))
    carry = entry.reshape(dp_count * micro_count, col_width)
    section_count = lax.axis_size("section")
    section_index = lax.axis_index("section")
    grad_cols = jnp.zeros_like(carry)
    grad_weight = jnp.zeros((col_width, width), jnp.float32)
    for section_turn in range(section_count):
        active_flag = section_count - 1 - section_turn
        inner = (carry * slope).astype(jnp.bfloat16)
        piece = lax.all_gather(inner, "dp", axis=1, tiled=True)
        back_sum = jnp.einsum("mj,ij->mi", piece, weight_rows, preferred_element_type=jnp.float32)
        weight_part = jnp.einsum("mi,mj->ij", input_cols, piece, preferred_element_type=jnp.float32)
        back_sum, layer_weight = (back_sum, weight_part)
        updated = carry + back_sum
        is_active = section_index == active_flag
        grad_cols = jnp.where(is_active, updated, grad_cols)
        grad_weight = jnp.where(is_active, layer_weight, grad_weight)
        if section_turn + 1 < section_count:
            carry = passed_along(updated, "section", -1)
    return (
        query_sums.reshape(blocks_here * row_block_count, width).astype(jnp.bfloat16),
        passage_out,
        grad_cols[None],
        grad_weight[None].astype(jnp.bfloat16),
    )


def solution(mesh):
    placed = (
        P(("section", "dp"), None),
        P("dp", None, None),
        P("section", None),
        P("section"),
        P(("section", "dp"), None),
        P("section", "dp", None),
        P("section", None, "dp"),
        P("section", None, "dp"),
    )
    return jax.shard_map(
        body,
        mesh=mesh,
        in_specs=placed,
        out_specs=(
            P(("section", "dp"), None),
            P("dp", None, None),
            P("section", None, "dp"),
            P("section", "dp", None),
        ),
        check_vma=False,
    )
```

profile of v0, /device:TPU:6, one launch (start us, length us, event | category | flops | bytes accessed | tf_op | source)
XLA Modules:
  0.0 731.4 jit_solution(10540011991136659404)
XLA Ops:
  1.8 15.6 %gather_fusion = bf16[192,2,3584]{2,0,1:T(8,128)(2,1)} fusion(bf16[2,64,3584]{2,1,0:T(8,128)(2,1)} %param.9, s32[1024]{0:T(1024)S(1)} %pad_clamp_fusion), kind=kCustom, calls=%fused_computation | custom fusion | bytes 5505792 | tf_op jit(solution)/shard_map/jit(_take)/gather | solution.py:31
  19.5 4.4 copy.29
  23.9 14.3 %all-to-all-start = ((bf16[2,192,3584]{2,0,1:T(2,128)(2,1)}), bf16[2,192,3584]{2,0,1:T(2,128)(2,1)}, u32[]{:S(2)}, u32[]{:S(2)}) async-start(bf16[2,192,3584]{2,0,1:T(2,128)(2,1)} %copy.29), calls=%async_computation | async-start | bytes 5505024 | tf_op jit(solution)/shard_map/all_to_all | solution.py:32
  40.0 61.0 %all-to-all-done = bf16[2,192,3584]{2,0,1:T(2,128)(2,1)} async-done(((bf16[2,192,3584]{2,0,1:T(2,128)(2,1)}), bf16[2,192,3584]{2,0,1:T(2,128)(2,1)}, u32[]{:S(2)}, u32[]{:S(2)}) %all-to-all-start) | async-done | bytes 2752544 | tf_op jit(solution)/shard_map/all_to_all | solution.py:32
  101.0 5.2 copy.30
  106.2 6.8 reshape.239
  118.5 8.0 %all-to-all-start.2 = ((f32[64,1,56]{2,1,0:T(1,128)}), f32[64,1,56]{2,1,0:T(1,128)S(1)}, u32[]{:S(2)}, u32[]{:S(2)}) async-start(f32[64,1,56]{2,1,0:T(1,128)} %bitcast.24), calls=%async_computation.2 | async-start | bytes 65536 | tf_op jit(solution)/shard_map/all_to_all | solution.py:71
  127.4 4.2 copy.33
  134.0 8.2 %all-to-all-start.1 = ((bf16[128,3,3584]{2,1,0:T(4,128)(2,1)}), bf16[128,3,3584]{2,1,0:T(4,128)(2,1)}, u32[]{:S(2)}, u32[]{:S(2)}) async-start(bf16[128,3,3584]{2,1,0:T(4,128)(2,1)} %copy.33), calls=%async_computation.1 | async-start | bytes 7340032 | tf_op jit(solution)/shard_map/all_to_all | solution.py:70
  142.3 124.3 %all_gather.24 = bf16[64,3584]{0,1:T(8,128)(2,1)S(1)} all-gather(bf16[64,56]{0,1:T(8,128)(2,1)S(1)} %fusion.38), channel_id=1, replica_groups=mesh['section'=8,'dp'=64] {'dp'}, dimensions={1}, use_global_device_ids=true | all-gather | bytes 465920 | tf_op jit(solution)/shard_map/all_gather | solution.py:96
  268.9 3.8 collective-permute-done
  272.7 48.2 %all_gather.25 = bf16[64,3584]{0,1:T(8,128)(2,1)S(1)} all-gather(bf16[64,56]{0,1:T(8,128)(2,1)S(1)} %multiply_convert_fusion.6), channel_id=1, replica_groups=mesh['section'=8,'dp'=64] {'dp'}, dimensions={1}, use_global_device_ids=true | all-gather | bytes 465920 | tf_op jit(solution)/shard_map/all_gather | solution.py:96
  327.0 49.7 %all_gather.26 = bf16[64,3584]{0,1:T(8,128)(2,1)S(1)} all-gather(bf16[64,56]{0,1:T(8,128)(2,1)S(1)} %multiply_convert_fusion.5), channel_id=1, replica_groups=mesh['section'=8,'dp'=64] {'dp'}, dimensions={1}, use_global_device_ids=true | all-gather | bytes 465920 | tf_op jit(solution)/shard_map/all_gather | solution.py:96
  378.9 3.8 collective-permute-done.2
  382.7 48.6 %all_gather.27 = bf16[64,3584]{0,1:T(8,128)(2,1)S(1)} all-gather(bf16[64,56]{0,1:T(8,128)(2,1)S(1)} %multiply_convert_fusion.4), channel_id=1, replica_groups=mesh['section'=8,'dp'=64] {'dp'}, dimensions={1}, use_global_device_ids=true | all-gather | bytes 465920 | tf_op jit(solution)/shard_map/all_gather | solution.py:96
  437.4 49.7 %all_gather.28 = bf16[64,3584]{0,1:T(8,128)(2,1)S(1)} all-gather(bf16[64,56]{0,1:T(8,128)(2,1)S(1)} %multiply_convert_fusion.3), channel_id=1, replica_groups=mesh['section'=8,'dp'=64] {'dp'}, dimensions={1}, use_global_device_ids=true | all-gather | bytes 465920 | tf_op jit(solution)/shard_map/all_gather | solution.py:96
  489.3 4.7 collective-permute-done.4
  494.1 48.2 %all_gather.29 = bf16[64,3584]{0,1:T(8,128)(2,1)S(1)} all-gather(bf16[64,56]{0,1:T(8,128)(2,1)S(1)} %multiply_convert_fusion.2), channel_id=1, replica_groups=mesh['section'=8,'dp'=64] {'dp'}, dimensions={1}, use_global_device_ids=true | all-gather | bytes 465920 | tf_op jit(solution)/shard_map/all_gather | solution.py:96
  544.5 5.0 collective-permute-done.5
  549.5 49.9 %all_gather.30 = bf16[64,3584]{0,1:T(8,128)(2,1)S(1)} all-gather(bf16[64,56]{0,1:T(8,128)(2,1)S(1)} %multiply_convert_fusion.1), channel_id=1, replica_groups=mesh['section'=8,'dp'=64] {'dp'}, dimensions={1}, use_global_device_ids=true | all-gather | bytes 465920 | tf_op jit(solution)/shard_map/all_gather | solution.py:96
  601.7 5.0 collective-permute-done.6
  606.7 48.2 %all_gather.31 = bf16[64,3584]{0,1:T(8,128)(2,1)S(1)} all-gather(bf16[64,56]{0,1:T(8,128)(2,1)S(1)} %multiply_convert_fusion), channel_id=1, replica_groups=mesh['section'=8,'dp'=64] {'dp'}, dimensions={1}, use_global_device_ids=true | all-gather | bytes 465920 | tf_op jit(solution)/shard_map/all_gather | solution.py:96
  657.2 4.4 copy.34
  662.2 69.0 %all-reduce.1 = bf16[2,64,3584]{2,1,0:T(8,128)(2,1)} all-reduce(f32[2,64,3584]{2,1,0:T(8,128)S(1)} %convolution_bitcast_fusion), channel_id=1, replica_groups=mesh['section'=8,'dp'=64] {'section'}, use_global_device_ids=true, to_apply=%region_4.5 | all-reduce | flops 458752 | bytes 2752512 | tf_op jit(solution)/shard_map/psum | solution.py:82
  (71 shorter events, 40.2 us)
Async XLA Ops:
  0.6 112.4 %copy-start = (bf16[128,3584]{1,0:T(8,128)(2,1)S(1)}, bf16[128,3584]{1,0:T(8,128)(2,1)}, u32[]{:S(2)}) copy-start(bf16[128,3584]{1,0:T(8,128)(2,1)} %param.8) | copy-start | bytes 2752516
  23.9 14.4 %copy-start.5 = (f32[128,384]{1,0:T(8,128)S(1)}, f32[128,384]{1,0:T(8,128)}, u32[]{:S(2)}) copy-start(f32[128,384]{1,0:T(8,128)} %param.12) | copy-start | bytes 589828
  23.9 14.5 %copy-start.6 = (s32[64]{0:T(128)S(1)}, s32[64]{0:T(128)}, u32[]{:S(2)}) copy-start(s32[64]{0:T(128)} %param.11) | copy-start | bytes 772
  23.9 77.0 %all-to-all-start = ((bf16[2,192,3584]{2,0,1:T(2,128)(2,1)}), bf16[2,192,3584]{2,0,1:T(2,128)(2,1)}, u32[]{:S(2)}, u32[]{:S(2)}) async-start(bf16[2,192,3584]{2,0,1:T(2,128)(2,1)} %copy.29), calls=%async_computation | async-start | bytes 5505024 | tf_op jit(solution)/shard_map/all_to_all | solution.py:32
  113.0 3.1 copy-start.1
  118.5 15.5 %all-to-all-start.2 = ((f32[64,1,56]{2,1,0:T(1,128)}), f32[64,1,56]{2,1,0:T(1,128)S(1)}, u32[]{:S(2)}, u32[]{:S(2)}) async-start(f32[64,1,56]{2,1,0:T(1,128)} %bitcast.24), calls=%async_computation.2 | async-start | bytes 65536 | tf_op jit(solution)/shard_map/all_to_all | solution.py:71
  131.6 10.7 %copy-start.4 = (bf16[1,64,56]{1,2,0:T(8,128)(2,1)S(1)}, bf16[1,64,56]{1,2,0:T(8,128)(2,1)}, u32[]{:S(2)}) copy-start(bf16[1,64,56]{1,2,0:T(8,128)(2,1)} %param.15) | copy-start | bytes 21508
  131.6 135.0 %copy-start.2 = (bf16[1,56,3584]{2,1,0:T(8,128)(2,1)S(1)}, bf16[1,56,3584]{2,1,0:T(8,128)(2,1)}, u32[]{:S(2)}) copy-start(bf16[1,56,3584]{2,1,0:T(8,128)(2,1)} %param.13) | copy-start | bytes 1204228
  131.6 136.6 %copy-start.3 = (bf16[1,64,56]{1,2,0:T(8,128)(2,1)S(1)}, bf16[1,64,56]{1,2,0:T(8,128)(2,1)}, u32[]{:S(2)}) copy-start(bf16[1,64,56]{1,2,0:T(8,128)(2,1)} %param.14) | copy-start | bytes 21508
  134.0 523.2 %all-to-all-start.1 = ((bf16[128,3,3584]{2,1,0:T(4,128)(2,1)}), bf16[128,3,3584]{2,1,0:T(4,128)(2,1)}, u32[]{:S(2)}, u32[]{:S(2)}) async-start(bf16[128,3,3584]{2,1,0:T(4,128)(2,1)} %copy.33), calls=%async_computation.1 | async-start | bytes 7340032 | tf_op jit(solution)/shard_map/all_to_all | solution.py:70
  266.9 5.8 collective-permute-start
  321.2 5.8 collective-permute-start.1
  376.9 5.8 collective-permute-start.2
  431.6 5.8 collective-permute-start.3
  487.4 6.7 collective-permute-start.4
  542.5 7.0 collective-permute-start.5
  599.7 7.0 collective-permute-start.6
where the time goes:
time: 742 us; the launch traced here: 731 us
  blocking collectives  536 us (72%)
  waiting for transfers between devices  93.2 us (13%)
  local copies, waits for them, and re-layouts  43.3 us (6%)
  starting transfers between devices  39.6 us (5%)
  matrix products  14.8 us (2%)
    all_gather x8, blocking collectives, body(): piece = lax.all_gather(inner, 'dp', axis=1, tiled=True)  467 us
    psum x1, blocking collectives, body(): passage_out = lax.psum(dense, 'section').astype(jnp.bfloat16)  69 us
    all_to_all x1, waiting for transfers between devices, body(): lax.all_to_all(outgoing, 'dp', split_axis=1, concat_axis=0, tiled=True)  61 us
    ppermute x7, waiting for transfers between devices, passed_along(): lax.ppermute(value, axis, [(source, source + steps) for source in range(i...  29.9 us
    gather x1, local copies, waits for them, and re-layouts, body(): outgoing = jnp.take(passages, all_slots, axis=1)  15.6 us
  transfers between devices with their start and end apart: 10, of which 9 were waited for; matrix products, arithmetic and copies ran while one was open for 2% of the time, Pallas kernels for 0%

commit v1 on v0

--- a/solution.py
+++ b/solution.py
@@ -10,6 +10,13 @@
     count = lax.axis_size(axis)
     initial, last = (max(0, -steps), min(count, count - steps))
     return lax.ppermute(value, axis, [(source, source + steps) for source in range(initial, last)])
+
+
+def gathered_columns(value, axis):
+    count = lax.axis_size(axis)
+    copies = jnp.broadcast_to(value[None], (count,) + value.shape)
+    pieces = lax.all_to_all(copies, axis, 0, 0, tiled=True)
+    return jnp.transpose(pieces, (1, 0, 2)).reshape(value.shape[0], count * value.shape[1])
 
 
 def soft_weights(logits, valid):
@@ -93,7 +100,7 @@
     for section_turn in range(section_count):
         active_flag = section_count - 1 - section_turn
         inner = (carry * slope).astype(jnp.bfloat16)
-        piece = lax.all_gather(inner, "dp", axis=1, tiled=True)
+        piece = gathered_columns(inner, "dp")
         back_sum = jnp.einsum("mj,ij->mi", piece, weight_rows, preferred_element_type=jnp.float32)
         weight_part = jnp.einsum("mi,mj->ij", input_cols, piece, preferred_element_type=jnp.float32)
         back_sum, layer_weight = (back_sum, weight_part)

time: 742 us -> 550 us (0.74)
  blocking collectives: 536 us -> 196 us
  waiting for transfers between devices: 93.2 us -> 171 us
  local copies, waits for them, and re-layouts: 43.3 us -> 87.5 us
  starting transfers between devices: 39.6 us -> 52.9 us
  matrix products: 14.8 us -> 26.2 us
    all_gather x8 -> x0, blocking collectives: 467 us -> none  [body(): piece = lax.all_gather(inner, 'dp', axis=1, tiled=True)]
    all_to_all x0 -> x6, blocking collectives: none -> 126 us  [the longest x5 110 us: gathered_columns(): pieces = lax.all_to_all(copies, axis, 0, 0, tiled=True)]
    all_to_all x1, waiting for transfers between devices: 0.01 us -> 66.1 us  [body(): lax.all_to_all(block_terms, 'dp', split_axis=0, concat_axis=1, tiled=True)]
    unnamed x16 -> x90, local copies, waits for them, and re-layouts: 1 us -> 41.3 us
    all_to_all x1 -> x3, starting transfers between devices: 8.02 us -> 22.3 us  [gathered_columns(): pieces = lax.all_to_all(copies, axis, 0, 0, tiled=True)]
    all_to_all x1 -> x3, waiting for transfers between devices: 2.42 us -> 15.2 us  [gathered_columns(): pieces = lax.all_to_all(copies, axis, 0, 0, tiled=True)]
  transfers between devices with their start and end apart: 10 -> 12, of which waited for: 9 -> 11; matrix products, arithmetic and copies ran while one was open for 2% -> 6% of each run, Pallas kernels for 0% -> 0%
where the time goes in v1:
time: 550 us; the launch traced here: 539 us
  blocking collectives  196 us (36%)
  waiting for transfers between devices  171 us (31%)
  local copies, waits for them, and re-layouts  87.5 us (16%)
  starting transfers between devices  52.9 us (10%)
  matrix products  26.2 us (5%)
    all_to_all x5, blocking collectives, gathered_columns(): pieces = lax.all_to_all(copies, axis, 0, 0, tiled=True)  110 us
    psum x1, blocking collectives, body(): passage_out = lax.psum(dense, 'section').astype(jnp.bfloat16)  70.3 us
    all_to_all x1, waiting for transfers between devices, body(): lax.all_to_all(block_terms, 'dp', split_axis=0, concat_axis=1, tiled=True)  66.1 us
    all_to_all x1, waiting for transfers between devices, body(): lax.all_to_all(outgoing, 'dp', split_axis=1, concat_axis=0, tiled=True)  61 us
    unnamed x90, local copies, waits for them, and re-layouts  41.3 us
    ppermute x7, waiting for transfers between devices, passed_along(): lax.ppermute(value, axis, [(source, source + steps) for source in range(i...  28.6 us
    all_to_all x3, starting transfers between devices, gathered_columns(): pieces = lax.all_to_all(copies, axis, 0, 0, tiled=True)  22.3 us
    gather x1, local copies, waits for them, and re-layouts, body(): outgoing = jnp.take(passages, all_slots, axis=1)  18.5 us
  transfers between devices with their start and end apart: 12, of which 11 were waited for; matrix products, arithmetic and copies ran while one was open for 6% of the time, Pallas kernels for 0%

profile of v1, /device:TPU:6, one launch (start us, length us, event | category | flops | bytes accessed | tf_op | source)
XLA Modules:
  0.0 539.1 jit_solution(13108721981685856505)
XLA Ops:
  1.8 18.5 %gather_fusion = bf16[192,2,3584]{2,0,1:T(8,128)(2,1)} fusion(bf16[2,64,3584]{2,1,0:T(8,128)(2,1)} %param.9, s32[1024]{0:T(1024)S(1)} %pad_clamp_fusion), kind=kCustom, calls=%fused_computation | custom fusion | bytes 5505792 | tf_op jit(solution)/shard_map/jit(_take)/gather | solution.py:38
  26.8 14.3 %all-to-all-start = ((bf16[2,192,3584]{2,0,1:T(2,128)(2,1)}), bf16[2,192,3584]{2,0,1:T(2,128)(2,1)}, u32[]{:S(2)}, u32[]{:S(2)}) async-start(bf16[2,192,3584]{2,0,1:T(2,128)(2,1)} %copy.45), calls=%async_computation | async-start | bytes 5505024 | tf_op jit(solution)/shard_map/all_to_all | solution.py:39
  42.9 61.0 %all-to-all-done = bf16[2,192,3584]{2,0,1:T(2,128)(2,1)} async-done(((bf16[2,192,3584]{2,0,1:T(2,128)(2,1)}), bf16[2,192,3584]{2,0,1:T(2,128)(2,1)}, u32[]{:S(2)}, u32[]{:S(2)}) %all-to-all-start) | async-done | bytes 2752544 | tf_op jit(solution)/shard_map/all_to_all | solution.py:39
  103.9 5.2 copy.46
  109.1 6.8 %reshape.273 = bf16[128,3,3584]{2,0,1:T(8,128)(2,1)} reshape(bf16[64,2,3,3584]{3,1,0,2:T(2,128)(2,1)} %copy.46) | data formatting | bytes 5505024 | tf_op jit(solution)/shard_map/reshape.6
  120.8 15.4 %all_to_all.82 = f32[64,1,56]{2,1,0:T(1,128)S(1)} all-to-all(f32[64,1,56]{2,1,0:T(1,128)S(1)} %bitcast.242), channel_id=1, replica_groups=mesh['section'=8,'dp'=64] {'dp'}, dimensions={0} | all-to-all | bytes 28672 | tf_op jit(solution)/shard_map/all_to_all | solution.py:78
  137.0 21.1 %all_to_all.83 = bf16[64,2,1792]{2,1,0:T(2,128)(2,1)S(1)} all-to-all(bf16[64,2,1792]{2,1,0:T(2,128)(2,1)S(1)} %reshape.300), channel_id=1, replica_groups=mesh['section'=8,'dp'=64] {'dp'}, dimensions={0} | all-to-all | bytes 917504 | tf_op jit(solution)/shard_map/all_to_all | solution.py:18
  160.3 4.5 collective-permute-done
  166.3 22.2 %all_to_all.84 = bf16[64,2,1792]{2,1,0:T(2,128)(2,1)S(1)} all-to-all(bf16[64,2,1792]{2,1,0:T(2,128)(2,1)} %reshape.302), channel_id=1, replica_groups=mesh['section'=8,'dp'=64] {'dp'}, dimensions={0} | all-to-all | bytes 917504 | tf_op jit(solution)/shard_map/all_to_all | solution.py:18
  196.6 22.3 %all_to_all.85 = bf16[64,2,1792]{2,1,0:T(2,128)(2,1)} all-to-all(bf16[64,2,1792]{2,1,0:T(2,128)(2,1)} %reshape.304), channel_id=1, replica_groups=mesh['section'=8,'dp'=64] {'dp'}, dimensions={0} | all-to-all | bytes 917504 | tf_op jit(solution)/shard_map/all_to_all | solution.py:18
  222.6 4.5 collective-permute-done.2
  231.0 22.3 %all_to_all.86 = bf16[64,2,1792]{2,1,0:T(2,128)(2,1)} all-to-all(bf16[64,2,1792]{2,1,0:T(2,128)(2,1)} %reshape.306), channel_id=1, replica_groups=mesh['section'=8,'dp'=64] {'dp'}, dimensions={0} | all-to-all | bytes 917504 | tf_op jit(solution)/shard_map/all_to_all | solution.py:18
  258.8 4.5 collective-permute-done.3
  267.2 22.3 %all_to_all.87 = bf16[64,2,1792]{2,1,0:T(2,128)(2,1)} all-to-all(bf16[64,2,1792]{2,1,0:T(2,128)(2,1)} %reshape.308), channel_id=1, replica_groups=mesh['section'=8,'dp'=64] {'dp'}, dimensions={0} | all-to-all | bytes 917504 | tf_op jit(solution)/shard_map/all_to_all | solution.py:18
  295.0 5.0 collective-permute-done.4
  304.0 7.2 %all-to-all-start.8 = ((bf16[64,2,1792]{2,1,0:T(2,128)(2,1)}), bf16[64,2,1792]{2,1,0:T(2,128)(2,1)}, u32[]{:S(2)}, u32[]{:S(2)}) async-start(bf16[64,2,1792]{2,1,0:T(2,128)(2,1)} %reshape.310), calls=%async_computation.8 | async-start | bytes 917504 | tf_op jit(solution)/shard_map/all_to_all | solution.py:18
  316.3 10.3 %all-to-all-done.8 = bf16[64,2,1792]{2,1,0:T(2,128)(2,1)} async-done(((bf16[64,2,1792]{2,1,0:T(2,128)(2,1)}), bf16[64,2,1792]{2,1,0:T(2,128)(2,1)}, u32[]{:S(2)}, u32[]{:S(2)}) %all-to-all-start.8) | async-done | bytes 458784 | tf_op jit(solution)/shard_map/all_to_all | solution.py:18
  326.6 7.0 %all-to-all-start.1 = ((bf16[128,3,3584]{2,1,0:T(4,128)(2,1)}), bf16[128,3,3584]{2,1,0:T(4,128)(2,1)}, u32[]{:S(2)}, u32[]{:S(2)}) async-start(bf16[128,3,3584]{2,1,0:T(4,128)(2,1)} %copy.49), calls=%async_computation.1 | async-start | bytes 7340032 | tf_op jit(solution)/shard_map/all_to_all | solution.py:77
  350.2 66.1 %all-to-all-done.1 = bf16[128,3,3584]{2,1,0:T(4,128)(2,1)} async-done(((bf16[128,3,3584]{2,1,0:T(4,128)(2,1)}), bf16[128,3,3584]{2,1,0:T(4,128)(2,1)}, u32[]{:S(2)}, u32[]{:S(2)}) %all-to-all-start.1) | async-done | bytes 2752544 | tf_op jit(solution)/shard_map/all_to_all | solution.py:77
  416.2 8.3 %all-to-all-start.9 = ((bf16[64,2,1792]{2,1,0:T(2,128)(2,1)}), bf16[64,2,1792]{2,1,0:T(2,128)(2,1)}, u32[]{:S(2)}, u32[]{:S(2)}) async-start(bf16[64,2,1792]{2,1,0:T(2,128)(2,1)} %reshape.312), calls=%async_computation.9 | async-start | bytes 917504 | tf_op jit(solution)/shard_map/all_to_all | solution.py:18
  428.8 6.0 %copy.50 = bf16[64,2,3,3584]{3,1,2,0:T(2,128)(2,1)} copy(bf16[64,2,3,3584]{3,2,1,0:T(4,128)(2,1)} %bitcast.19) | data formatting | bytes 5505024 | tf_op jit(solution)/shard_map/all_to_all | solution.py:77
  434.8 4.9 all-to-all-done.9
  453.8 6.8 %all-to-all-start.10 = ((bf16[64,2,1792]{2,1,0:T(2,128)(2,1)}), bf16[64,2,1792]{2,1,0:T(2,128)(2,1)}, u32[]{:S(2)}, u32[]{:S(2)}) async-start(bf16[64,2,1792]{2,1,0:T(2,128)(2,1)} %reshape.314), calls=%async_computation.10 | async-start | bytes 917504 | tf_op jit(solution)/shard_map/all_to_all | solution.py:18
  460.6 70.3 %all-reduce.1 = bf16[2,64,3584]{2,1,0:T(8,128)(2,1)} all-reduce(f32[2,64,3584]{2,1,0:T(8,128)} %convolution_bitcast_fusion), channel_id=1, replica_groups=mesh['section'=8,'dp'=64] {'section'}, use_global_device_ids=true, to_apply=%region_4.5 | all-reduce | flops 458752 | bytes 2752512 | tf_op jit(solution)/shard_map/psum | solution.py:89
  (147 shorter events, 101.0 us)
Async XLA Ops:
  0.6 115.2 %copy-start = (bf16[128,3584]{1,0:T(8,128)(2,1)S(1)}, bf16[128,3584]{1,0:T(8,128)(2,1)}, u32[]{:S(2)}) copy-start(bf16[128,3584]{1,0:T(8,128)(2,1)} %param.8) | copy-start | bytes 2752516
  1.6 18.7 %copy-start.29 = (s32[192]{0:T(256)}, s32[192]{0:T(256)S(1)}, u32[]{:S(2)}) copy-start(s32[192]{0:T(256)S(1)} %reshape.271) | copy-start | bytes 2308
  26.8 14.3 %copy-start.10 = (f32[128,384]{1,0:T(8,128)S(1)}, f32[128,384]{1,0:T(8,128)}, u32[]{:S(2)}) copy-start(f32[128,384]{1,0:T(8,128)} %param.12) | copy-start | bytes 589828
  26.8 14.5 %copy-start.31 = (s32[64]{0:T(128)S(1)}, s32[64]{0:T(128)}, u32[]{:S(2)}) copy-start(s32[64]{0:T(128)} %param.11) | copy-start | bytes 772
  26.8 77.0 %all-to-all-start = ((bf16[2,192,3584]{2,0,1:T(2,128)(2,1)}), bf16[2,192,3584]{2,0,1:T(2,128)(2,1)}, u32[]{:S(2)}, u32[]{:S(2)}) async-start(bf16[2,192,3584]{2,0,1:T(2,128)(2,1)} %copy.45), calls=%async_computation | async-start | bytes 5505024 | tf_op jit(solution)/shard_map/all_to_all | solution.py:39
  119.0 17.2 %copy-start.8 = (bf16[1,64,56]{1,2,0:T(8,128)(2,1)S(1)}, bf16[1,64,56]{1,2,0:T(8,128)(2,1)}, u32[]{:S(2)}) copy-start(bf16[1,64,56]{1,2,0:T(8,128)(2,1)} %param.15) | copy-start | bytes 21508
  120.6 38.0 %copy-start.2 = (bf16[1,56,3584]{2,1,0:T(8,128)(2,1)S(1)}, bf16[1,56,3584]{2,1,0:T(8,128)(2,1)}, u32[]{:S(2)}) copy-start(bf16[1,56,3584]{2,1,0:T(8,128)(2,1)} %param.13) | copy-start | bytes 1204228
  158.7 7.6 %copy-start.6 = (bf16[64,56,64]{2,1,0:T(8,128)(2,1)}, bf16[64,56,64]{2,1,0:T(8,128)(2,1)S(1)}, u32[]{:S(2)}) copy-start(bf16[64,56,64]{2,1,0:T(8,128)(2,1)S(1)} %reshape.301) | copy-start | bytes 1376260
  159.0 5.8 %collective-permute-start = (f32[64,56]{0,1:T(8,128)S(1)}, f32[64,56]{0,1:T(8,128)S(1)}, u32[]{:S(2)}, u32[]{:S(2)}) collective-permute-start(f32[64,56]{0,1:T(8,128)S(1)} %convolution_add_fusion.7), channel_id=1, source_target_pairs={{64,0},{128,64},{192,128},{256,192},{320,256},{384,320},{448,384},... | collective-permute-start | bytes 43016 | tf_op jit(solution)/shard_map/ppermute | solution.py:12
  189.3 5.8 %collective-permute-start.1 = (f32[64,56]{0,1:T(8,128)S(1)}, f32[64,56]{0,1:T(8,128)S(1)}, u32[]{:S(2)}, u32[]{:S(2)}) collective-permute-start(f32[64,56]{0,1:T(8,128)S(1)} %convolution_add_fusion.6), channel_id=1, source_target_pairs={{64,0},{128,64},{192,128},{256,192},{320,256},{384,320},{448,384},... | collective-permute-start | bytes 43016 | tf_op jit(solution)/shard_map/ppermute | solution.py:12
  221.3 5.8 %collective-permute-start.2 = (f32[64,56]{0,1:T(8,128)S(1)}, f32[64,56]{0,1:T(8,128)S(1)}, u32[]{:S(2)}, u32[]{:S(2)}) collective-permute-start(f32[64,56]{0,1:T(8,128)S(1)} %convolution_add_fusion.5), channel_id=1, source_target_pairs={{64,0},{128,64},{192,128},{256,192},{320,256},{384,320},{448,384},... | collective-permute-start | bytes 43016 | tf_op jit(solution)/shard_map/ppermute | solution.py:12
  257.5 5.8 %collective-permute-start.3 = (f32[64,56]{0,1:T(8,128)S(1)}, f32[64,56]{0,1:T(8,128)S(1)}, u32[]{:S(2)}, u32[]{:S(2)}) collective-permute-start(f32[64,56]{0,1:T(8,128)S(1)} %convolution_add_fusion.4), channel_id=1, source_target_pairs={{64,0},{128,64},{192,128},{256,192},{320,256},{384,320},{448,384},... | collective-permute-start | bytes 43016 | tf_op jit(solution)/shard_map/ppermute | solution.py:12
  293.7 6.3 %collective-permute-start.4 = (f32[64,56]{0,1:T(8,128)S(1)}, f32[64,56]{0,1:T(8,128)S(1)}, u32[]{:S(2)}, u32[]{:S(2)}) collective-permute-start(f32[64,56]{0,1:T(8,128)S(1)} %convolution_add_fusion.3), channel_id=1, source_target_pairs={{64,0},{128,64},{192,128},{256,192},{320,256},{384,320},{448,384},... | collective-permute-start | bytes 43016 | tf_op jit(solution)/shard_map/ppermute | solution.py:12
  304.0 22.6 %all-to-all-start.8 = ((bf16[64,2,1792]{2,1,0:T(2,128)(2,1)}), bf16[64,2,1792]{2,1,0:T(2,128)(2,1)}, u32[]{:S(2)}, u32[]{:S(2)}) async-start(bf16[64,2,1792]{2,1,0:T(2,128)(2,1)} %reshape.310), calls=%async_computation.8 | async-start | bytes 917504 | tf_op jit(solution)/shard_map/all_to_all | solution.py:18
  326.6 89.6 %all-to-all-start.1 = ((bf16[128,3,3584]{2,1,0:T(4,128)(2,1)}), bf16[128,3,3584]{2,1,0:T(4,128)(2,1)}, u32[]{:S(2)}, u32[]{:S(2)}) async-start(bf16[128,3,3584]{2,1,0:T(4,128)(2,1)} %copy.49), calls=%async_computation.1 | async-start | bytes 7340032 | tf_op jit(solution)/shard_map/all_to_all | solution.py:77
  337.9 7.0 %collective-permute-start.5 = (f32[64,56]{0,1:T(8,128)S(1)}, f32[64,56]{0,1:T(8,128)S(1)}, u32[]{:S(2)}, u32[]{:S(2)}) collective-permute-start(f32[64,56]{0,1:T(8,128)S(1)} %convolution_add_fusion.2), channel_id=1, source_target_pairs={{64,0},{128,64},{192,128},{256,192},{320,256},{384,320},{448,384},... | collective-permute-start | bytes 43016 | tf_op jit(solution)/shard_map/ppermute | solution.py:12
  416.2 23.4 %all-to-all-start.9 = ((bf16[64,2,1792]{2,1,0:T(2,128)(2,1)}), bf16[64,2,1792]{2,1,0:T(2,128)(2,1)}, u32[]{:S(2)}, u32[]{:S(2)}) async-start(bf16[64,2,1792]{2,1,0:T(2,128)(2,1)} %reshape.312), calls=%async_computation.9 | async-start | bytes 917504 | tf_op jit(solution)/shard_map/all_to_all | solution.py:18
  428.8 12.9 %copy-start.14 = (f32[64,56]{0,1:T(8,128)S(1)}, f32[64,56]{0,1:T(8,128)}, u32[]{:S(2)}) copy-start(f32[64,56]{0,1:T(8,128)} %copy-done.13) | copy-start | bytes 43012
  434.8 8.6 %copy-start.30 = (s32[192]{0:T(256)S(1)}, s32[192]{0:T(256)}, u32[]{:S(2)}) copy-start(s32[192]{0:T(256)} %copy-done.29) | copy-start | bytes 2308
  441.8 7.4 %copy-start.9 = (bf16[1,64,56]{1,2,0:T(8,128)(2,1)S(1)}, bf16[1,64,56]{1,2,0:T(8,128)(2,1)}, u32[]{:S(2)}) copy-start(bf16[1,64,56]{1,2,0:T(8,128)(2,1)} %param.15) | copy-start | bytes 21508
  442.1 7.2 %copy-start.27 = (f32[64,56]{0,1:T(8,128)}, f32[64,56]{0,1:T(8,128)S(1)}, u32[]{:S(2)}) copy-start(f32[64,56]{0,1:T(8,128)S(1)} %convolution_add_fusion.1) | copy-start | bytes 43012
  442.1 7.1 %collective-permute-start.6 = (f32[64,56]{0,1:T(8,128)S(1)}, f32[64,56]{0,1:T(8,128)S(1)}, u32[]{:S(2)}, u32[]{:S(2)}) collective-permute-start(f32[64,56]{0,1:T(8,128)S(1)} %convolution_add_fusion.1), channel_id=1, source_target_pairs={{64,0},{128,64},{192,128},{256,192},{320,256},{384,320},{448,384},... | collective-permute-start | bytes 43016 | tf_op jit(solution)/shard_map/ppermute | solution.py:12
  450.8 80.0 %copy-start.5 = (bf16[64,56,64]{2,1,0:T(8,128)(2,1)S(1)}, bf16[64,56,64]{2,1,0:T(8,128)(2,1)}, u32[]{:S(2)}) copy-start(bf16[64,56,64]{2,1,0:T(8,128)(2,1)} %reshape.311) | copy-start | bytes 1376260
  453.8 80.0 %all-to-all-start.10 = ((bf16[64,2,1792]{2,1,0:T(2,128)(2,1)}), bf16[64,2,1792]{2,1,0:T(2,128)(2,1)}, u32[]{:S(2)}, u32[]{:S(2)}) async-start(bf16[64,2,1792]{2,1,0:T(2,128)(2,1)} %reshape.314), calls=%async_computation.10 | async-start | bytes 917504 | tf_op jit(solution)/shard_map/all_to_all | solution.py:18
  (20 other events, 84.9 us)
